TPU v7x, 256 devices: a whole 4x4x8 slice. The times are simulated.
256 devices in a mesh: seq: 32 (over z, y), tp: 8 (over x, core).
Axes of the slice: x: 4, y: 4, z: 8, core: 2. Of those that a mesh axis runs over, the one named last changes fastest.
Arguments:
- tokens: bfloat16 [384, 4096], P(None, 'seq'), may hold values from -30 to 30
- ln_first_gain: bfloat16 [4096], P('seq'), may hold values from 0.099609375 to 1.8984375
- w_qkv: bfloat16 [4096, 3, 4096], P('seq', None, 'tp'), may hold values from -0.25 to 0.25
- w_out: bfloat16 [4096, 4096], P('tp', 'seq'), may hold values from -1 to 1
- ln_second_gain: bfloat16 [4096], P('seq'), may hold values from 0.099609375 to 1.8984375
- w_up: bfloat16 [4096, 16384], P('seq', 'tp'), may hold values from -0.09375 to 0.09375
- w_down: bfloat16 [16384, 4096], P('tp', 'seq'), may hold values from -0.09375 to 0.09375
- prompt_key: bfloat16 [8, 16384, 4096], P(None, 'seq', 'tp'), may hold values from -200 to 200
- prompt_val: bfloat16 [8, 16384, 4096], P(None, 'seq', 'tp'), may hold values from -20 to 20
- cont_key: bfloat16 [96, 256, 4096], P('seq', None, 'tp'), may hold values from -18 to 18
- cont_val: bfloat16 [96, 256, 4096], P('seq', None, 'tp'), may hold values from -20 to 20
- group_ids: int32 [96], replicated, may hold values from 0 to 7, as said below
- prompt_len: int32 [8], replicated, may hold values from 1 to 16384, as said below
- cont_len: int32 [96], replicated, may hold values from 0 to 252, as said below
Outputs:
- layer_out: bfloat16 [384, 4096], P(None, 'seq')
Inputs may be any that keep to these rules, and one draw needn't show every extreme that they name: `group_ids`: each of the 8 groups is named by exactly 12 requests. `prompt_len`: one group's prompt has exactly 16384 positions. `cont_len`: some request has exactly 252 filled slots.
All inputs are finite; a program needn't handle non-finite values.
Results may differ from a plain program's by a relative error of at most 0.013.
The roundings to bfloat16 on the way count: a program that leaves them out, or rounds other values in their place, can miss the bound.
Values may be sent and summed in bfloat16 or wider, within the bound.
No kernel may reach another device: no remote copies, remote signals or barrier semaphores. Data moves between devices by JAX's collectives and lax.ppermute only.
A program may use at most 128 MiB of HBM per device.

v0:
```python
import math
import jax
import jax.numpy as jnp
from jax import lax
from jax.sharding import PartitionSpec as P

D = 4096
HEADS = 32
HD = 128
NEW = 4
NEG_FILL = -1e30
NORM_EPS = 1e-05


def finish_norm(values, row_sum, row_square, gain):
    mean_row = row_sum / D
    variance = row_square / D - mean_row * mean_row
    scaled = (values - mean_row[:, None]) * lax.rsqrt(variance + NORM_EPS)[:, None]
    return (scaled * gain.astype(jnp.float32)[None, :]).astype(jnp.bfloat16)


def combine_parts(earlier, later):
    merged_top = jnp.maximum(earlier[0], later[0])
    left_factor = jnp.exp(earlier[0] - merged_top)
    right_factor = jnp.exp(later[0] - merged_top)
    merged_sum = earlier[1] * left_factor + later[1] * right_factor
    merged_acc = earlier[2] * left_factor[..., None] + later[2] * right_factor[..., None]
    return (merged_top, merged_sum, merged_acc)


def body(
    tokens,
    ln_first_gain,
    w_qkv,
    w_out,
    ln_second_gain,
    w_up,
    w_down,
    prompt_key,
    prompt_val,
    cont_key,
    cont_val,
    group_ids,
    prompt_len,
    cont_len,
):
    row_count = tokens.shape[0]
    seq_index = lax.axis_index("seq")
    tp_index = lax.axis_index("tp")
    feat_width = w_qkv.shape[2]
    local_heads = feat_width // HD
    home_requests = cont_key.shape[0]
    home_rows = home_requests * NEW
    requests = row_count // NEW
    groups = prompt_key.shape[0]
    block_len = prompt_key.shape[1]
    slots = cont_key.shape[1]
    score_scale = 1.0 / math.sqrt(HD)
    token_float = tokens.astype(jnp.float32)
    first_sums = lax.psum((jnp.sum(token_float, 1), jnp.sum(token_float * token_float, 1)), "seq")
    normed = finish_norm(token_float, first_sums[0], first_sums[1], ln_first_gain)
    w_flat = w_qkv.reshape(w_qkv.shape[0], 3 * feat_width)
    partial_qkv = jnp.dot(normed, w_flat, preferred_element_type=jnp.float32)
    full_qkv = lax.psum(partial_qkv, "seq").astype(jnp.bfloat16)
    query = full_qkv[:, :feat_width]
    own_slice = lax.dynamic_slice_in_dim(full_qkv, seq_index * home_rows, home_rows, 0)
    key_new = own_slice[:, feat_width : 2 * feat_width]
    val_new = own_slice[:, 2 * feat_width :]
    head_first = (tp_index * local_heads).astype(jnp.float32)
    slopes = jnp.exp2(
        -8.0 * (head_first + jnp.arange(local_heads, dtype=jnp.float32) + 1.0) / HEADS
    )
    members = jnp.argsort(group_ids, stable=True).reshape(groups, requests // groups)
    inverse = jnp.argsort(members.reshape(-1))
    group_match = group_ids[:, None] == jnp.arange(groups, dtype=jnp.int32)[None, :]
    req_prompt = jnp.sum(jnp.where(group_match, prompt_len[None, :], 0), 1)
    query_pos = (req_prompt + cont_len)[:, None] + jnp.arange(NEW, dtype=jnp.int32)[None, :]
    query_req = query.reshape(requests, NEW, local_heads, HD)
    group_query = query_req[members].reshape(groups, -1, local_heads, HD)
    group_pos = query_pos[members].reshape(groups, -1)
    key_slab = prompt_key.reshape(groups, block_len, local_heads, HD)
    val_slab = prompt_val.reshape(groups, block_len, local_heads, HD)
    key_pos = seq_index * block_len + jnp.arange(block_len, dtype=jnp.int32)
    scores = jnp.einsum(
        "gqhd,gphd->ghqp", group_query, key_slab, preferred_element_type=jnp.float32
    )
    distance = (key_pos[None, None, :] - group_pos[:, :, None]).astype(jnp.float32)
    scores = scores * score_scale + slopes[None, :, None, None] * distance[:, None, :, :]
    is_live = (key_pos[None, :] < prompt_len[:, None])[:, None, None, :]
    block_top = jnp.max(jnp.where(is_live, scores, NEG_FILL), -1)
    weights = jnp.where(is_live, jnp.exp(scores - block_top[..., None]), 0.0)
    block_sum = jnp.sum(weights, -1)
    block_acc = jnp.einsum(
        "ghqp,gphd->gqhd",
        weights.astype(jnp.bfloat16),
        val_slab,
        preferred_element_type=jnp.float32,
    )
    prompt_top = (
        jnp.transpose(block_top, (0, 2, 1))
        .reshape(requests, NEW, local_heads)[inverse]
        .reshape(row_count, local_heads)
    )
    prompt_sum = (
        jnp.transpose(block_sum, (0, 2, 1))
        .reshape(requests, NEW, local_heads)[inverse]
        .reshape(row_count, local_heads)
    )
    prompt_acc = block_acc.reshape(requests, NEW, local_heads, HD)[inverse].reshape(
        row_count, local_heads, HD
    )
    home_query = lax.dynamic_slice_in_dim(query_req, seq_index * home_requests, home_requests, 0)
    home_pos = lax.dynamic_slice_in_dim(query_pos, seq_index * home_requests, home_requests, 0)
    home_prompt = lax.dynamic_slice_in_dim(req_prompt, seq_index * home_requests, home_requests, 0)
    home_filled = lax.dynamic_slice_in_dim(cont_len, seq_index * home_requests, home_requests, 0)
    cache_keys = cont_key.reshape(home_requests, slots, local_heads, HD)
    cache_vals = cont_val.reshape(home_requests, slots, local_heads, HD)
    slot_index = jnp.arange(slots, dtype=jnp.int32)
    cache_pos = home_prompt[:, None] + slot_index[None, :]
    cache_scores = (
        jnp.einsum("rjhd,rkhd->rhjk", home_query, cache_keys, preferred_element_type=jnp.float32)
        * score_scale
    )
    cache_scores = cache_scores + slopes[None, :, None, None] * (
        cache_pos[:, None, None, :] - home_pos[:, None, :, None]
    ).astype(jnp.float32)
    cache_live = (slot_index[None, :] < home_filled[:, None])[:, None, None, :]
    fresh_keys = key_new.reshape(home_requests, NEW, local_heads, HD)
    fresh_vals = val_new.reshape(home_requests, NEW, local_heads, HD)
    steps_new = jnp.arange(NEW, dtype=jnp.int32)
    fresh_dist = (steps_new[None, :] - steps_new[:, None]).astype(jnp.float32)
    fresh_scores = (
        jnp.einsum("rjhd,rkhd->rhjk", home_query, fresh_keys, preferred_element_type=jnp.float32)
        * score_scale
    )
    fresh_scores = fresh_scores + slopes[None, :, None, None] * fresh_dist[None, None, :, :]
    fresh_live = (steps_new[None, :] <= steps_new[:, None])[None, None, :, :]
    home_top = jnp.maximum(
        jnp.max(jnp.where(cache_live, cache_scores, NEG_FILL), -1),
        jnp.max(jnp.where(fresh_live, fresh_scores, NEG_FILL), -1),
    )
    cache_weights = jnp.where(cache_live, jnp.exp(cache_scores - home_top[..., None]), 0.0)
    fresh_weights = jnp.where(fresh_live, jnp.exp(fresh_scores - home_top[..., None]), 0.0)
    home_sum = jnp.sum(cache_weights, -1) + jnp.sum(fresh_weights, -1)
    home_acc = jnp.einsum(
        "rhjk,rkhd->rjhd",
        cache_weights.astype(jnp.bfloat16),
        cache_vals,
        preferred_element_type=jnp.float32,
    )
    home_acc = home_acc + jnp.einsum(
        "rhjk,rkhd->rjhd",
        fresh_weights.astype(jnp.bfloat16),
        fresh_vals,
        preferred_element_type=jnp.float32,
    )
    home_top = jnp.transpose(home_top, (0, 2, 1)).reshape(home_rows, local_heads)
    home_sum = jnp.transpose(home_sum, (0, 2, 1)).reshape(home_rows, local_heads)
    home_acc = home_acc.reshape(home_rows, local_heads, HD)
    row_start = seq_index * home_rows
    home_part = (
        lax.dynamic_update_slice_in_dim(
            jnp.full((row_count, local_heads), NEG_FILL, jnp.float32), home_top, row_start, 0
        ),
        lax.dynamic_update_slice_in_dim(
            jnp.zeros((row_count, local_heads), jnp.float32), home_sum, row_start, 0
        ),
        lax.dynamic_update_slice_in_dim(
            jnp.zeros((row_count, local_heads, HD), jnp.float32), home_acc, row_start, 0
        ),
    )
    local_part = combine_parts((prompt_top, prompt_sum, prompt_acc), home_part)
    global_top = lax.pmax(local_part[0], "seq")
    factor = jnp.exp(local_part[0] - global_top)
    merged_sum, merged_acc = lax.psum(
        (local_part[1] * factor, local_part[2] * factor[..., None]), "seq"
    )
    attended = (
        (merged_acc / merged_sum[..., None]).reshape(row_count, feat_width).astype(jnp.bfloat16)
    )
    attn_sum = lax.psum(jnp.dot(attended, w_out, preferred_element_type=jnp.float32), "tp")
    hidden_state = token_float + attn_sum
    second_sums = lax.psum(
        (jnp.sum(hidden_state, 1), jnp.sum(hidden_state * hidden_state, 1)), "seq"
    )
    second_normed = finish_norm(hidden_state, second_sums[0], second_sums[1], ln_second_gain)
    up_sum = lax.psum(jnp.dot(second_normed, w_up, preferred_element_type=jnp.float32), "seq")
    activated = jax.nn.gelu(up_sum, approximate=False).astype(jnp.bfloat16)
    down_part = jnp.dot(activated, w_down, preferred_element_type=jnp.float32)
    down_sum = lax.psum(down_part.astype(jnp.bfloat16), "tp").astype(jnp.float32)
    return (hidden_state + down_sum).astype(jnp.bfloat16)


def solution(mesh):
    in_specs = (
        P(None, "seq"),
        P("seq"),
        P("seq", None, "tp"),
        P("tp", "seq"),
        P("seq"),
        P("seq", "tp"),
        P("tp", "seq"),
        P(None, "seq", "tp"),
        P(None, "seq", "tp"),
        P("seq", None, "tp"),
        P("seq", None, "tp"),
        P(),
        P(),
        P(),
    )
    out_specs = P(None, "seq")
    return jax.shard_map(body, mesh=mesh, in_specs=in_specs, out_specs=out_specs, check_vma=False)
```

profile of v0, /device:TPU:8, one launch (start us, length us, event | category | flops | bytes accessed | tf_op | source)
XLA Modules:
  0.0 878.5 jit_solution(7815176637591646648)
XLA Ops:
  8.7 1.3 dynamic_slice.15
  9.9 1.2 convert_element_type.71
  11.2 3.2 sort.34
  16.3 1.2 gather_fusion.1
  17.5 1.2 copy.124
  18.7 73.8 %all-reduce.1 = (f32[384]{0:T(512)S(1)}, f32[384]{0:T(512)S(1)}) all-reduce(f32[384]{0:T(512)S(1)} %get-tuple-element.12, f32[384]{0:T(512)S(1)} %get-tuple-element.11), channel_id=1, replica_groups=mesh['seq'=32,'tp'=8] {'seq'}, use_global_device_ids=true, to_apply=%region_3.0 | all-reduce | flops 768 | bytes 6144 | tf_op jit(solution)/shard_map/psum | solution.py:60
  92.5 1.4 fusion.48
  93.9 165.3 %all-reduce.15 = bf16[384,1536]{1,0:T(8,128)(2,1)} all-reduce(f32[384,1536]{1,0:T(8,128)S(1)} %fusion.48), channel_id=1, replica_groups=mesh['seq'=32,'tp'=8] {'seq'}, use_global_device_ids=true, to_apply=%region_4.0 | all-reduce | flops 589824 | bytes 3538944 | tf_op jit(solution)/shard_map/psum | solution.py:64
  262.1 3.2 sort.35
  270.3 4.0 select_reduce_fusion
  275.4 1.5 fusion.27
  277.0 1.1 gather_fusion.2
  280.5 73.7 %pmax.7 = f32[384,4]{0,1:T(4,128)S(1)} all-reduce(f32[384,4]{0,1:T(4,128)S(1)} %max.18), channel_id=1, replica_groups=mesh['seq'=32,'tp'=8] {'seq'}, use_global_device_ids=true, to_apply=%region_11.12 | all-reduce | flops 1536 | bytes 12288 | tf_op jit(solution)/shard_map/pmax | solution.py:173
  354.8 1.5 add_multiply_fusion
  356.4 72.8 %psum.74 = f32[384,4]{0,1:T(4,128)S(1)} all-reduce(f32[384,4]{0,1:T(4,128)S(1)} %get-tuple-element.17), channel_id=1, replica_groups=mesh['seq'=32,'tp'=8] {'seq'}, use_global_device_ids=true, to_apply=%region_16.17 | all-reduce | flops 1536 | bytes 12288 | tf_op jit(solution)/shard_map/psum | solution.py:175
  429.3 72.5 %all-reduce.8.cloned.1.call-done = f32[384,4,128]{2,0,1:T(8,128)} async-done(((f32[384,4,128]{2,0,1:T(8,128)}), f32[384,4,128]{2,0,1:T(8,128)}) %all-reduce.8.cloned.1.call-update) | async-done | bytes 786448 | tf_op jit(solution)/shard_map/psum | solution.py:175
  501.8 1.4 divide_convert_fusion
  504.5 63.9 %all-reduce.10.cloned.1.call-done = f32[384,128]{1,0:T(8,128)} async-done(((f32[384,128]{1,0:T(8,128)}), f32[384,128]{1,0:T(8,128)}) %all-reduce.10.cloned.1.call-update) | async-done | bytes 196624 | tf_op jit(solution)/shard_map/psum | solution.py:181
  569.5 71.2 %all-reduce = (f32[384]{0:T(512)S(1)}, f32[384]{0:T(512)S(1)}) all-reduce(f32[384]{0:T(512)S(1)} %get-tuple-element.10, f32[384]{0:T(512)S(1)} %get-tuple-element.9), channel_id=1, replica_groups=mesh['seq'=32,'tp'=8] {'seq'}, use_global_device_ids=true, to_apply=%region_21.22 | all-reduce | flops 768 | bytes 6144 | tf_op jit(solution)/shard_map/psum | solution.py:183
  640.7 3.3 fusion.47
  644.3 154.8 %all-reduce.12.cloned.1.call-done = f32[384,2048]{1,0:T(8,128)} async-done(((f32[384,2048]{1,0:T(8,128)}), f32[384,2048]{1,0:T(8,128)}) %all-reduce.12.cloned.1.call-update) | async-done | bytes 3145744 | tf_op jit(solution)/shard_map/psum | solution.py:187
  799.1 9.0 %fusion.32 = bf16[384,128]{1,0:T(8,128)(2,1)} fusion(bf16[2048,128]{1,0:T(8,128)(2,1)S(1)} %copy-done.8, f32[384,2048]{1,0:T(8,128)} %all-reduce.12.cloned.1.call-done), kind=kOutput, calls=%fused_computation.43 | convolution fusion | flops 252493824 | bytes 3768320 | tf_op jit(solution)/shard_map/dot_general | solution.py:189
  808.2 62.2 %all-reduce.14.cloned.1.call-done = bf16[384,128]{1,0:T(8,128)(2,1)} async-done(((bf16[384,128]{1,0:T(8,128)(2,1)}), bf16[384,128]{1,0:T(8,128)(2,1)}) %all-reduce.14.cloned.1.call-update) | async-done | bytes 98320 | tf_op jit(solution)/shard_map/psum | solution.py:190
  870.4 1.6 add_convert_fusion
  (97 shorter events, 18.5 us)
Async XLA Ops:
  6.5 262.4 %copy-start = (bf16[3,256,512]{2,1,0:T(8,128)(2,1)S(1)}, bf16[3,256,512]{2,1,0:T(8,128)(2,1)}, u32[]{:S(2)}) copy-start(bf16[3,256,512]{2,1,0:T(8,128)(2,1)} %param.23) | copy-start | bytes 2359300
  6.5 495.3 %all-reduce.8.cloned.1.call-start = ((), (), s32[]{:S(2)}) async-start(), calls=%async_computation | async-start | bytes 1572864 | tf_op jit(solution)/shard_map/psum | solution.py:175
  14.4 0.5 copy-start.5
  259.2 10.4 %copy-start.7 = (bf16[3,256,512]{2,1,0:T(8,128)(2,1)S(1)}, bf16[3,256,512]{2,1,0:T(8,128)(2,1)}, u32[]{:S(2)}) copy-start(bf16[3,256,512]{2,1,0:T(8,128)(2,1)} %param.24) | copy-start | bytes 2359300
  270.3 5.1 copy-start.6
  280.1 223.3 %copy-start.4 = (bf16[512,128]{1,0:T(8,128)(2,1)S(1)}, bf16[512,128]{1,0:T(8,128)(2,1)}, u32[]{:S(2)}) copy-start(bf16[512,128]{1,0:T(8,128)(2,1)} %param.17) | copy-start | bytes 393220
  354.6 149.9 %copy-start.9 = (bf16[128]{0:T(256)(128)(2,1)S(1)}, bf16[128]{0:T(256)(128)(2,1)}, u32[]{:S(2)}) copy-start(bf16[128]{0:T(256)(128)(2,1)} %param.18) | copy-start | bytes 772
  354.6 213.8 %copy-start.1 = (bf16[384,128]{1,0:T(8,128)(2,1)S(1)}, bf16[384,128]{1,0:T(8,128)(2,1)}, u32[]{:S(2)}) copy-start(bf16[384,128]{1,0:T(8,128)(2,1)} %param.14) | copy-start | bytes 294916
  354.8 285.9 %copy-start.3 = (bf16[128,2048]{1,0:T(8,128)(2,1)S(1)}, bf16[128,2048]{1,0:T(8,128)(2,1)}, u32[]{:S(2)}) copy-start(bf16[128,2048]{1,0:T(8,128)(2,1)} %param.19) | copy-start | bytes 1572868
  356.4 212.0 %all-reduce.10.cloned.1.call-start = ((), (), s32[]{:S(2)}) async-start(), calls=%async_computation.1 | async-start | bytes 393216 | tf_op jit(solution)/shard_map/psum | solution.py:181
  504.4 294.6 %all-reduce.12.cloned.1.call-start = ((), (), s32[]{:S(2)}) async-start(), calls=%async_computation.2 | async-start | bytes 6291456 | tf_op jit(solution)/shard_map/psum | solution.py:187
  640.7 158.4 %copy-start.8 = (bf16[2048,128]{1,0:T(8,128)(2,1)S(1)}, bf16[2048,128]{1,0:T(8,128)(2,1)}, u32[]{:S(2)}) copy-start(bf16[2048,128]{1,0:T(8,128)(2,1)} %param.20) | copy-start | bytes 1572868
  644.1 226.3 %copy-start.2 = (f32[384,128]{1,0:T(8,128)S(1)}, f32[384,128]{1,0:T(8,128)}, u32[]{:S(2)}) copy-start(f32[384,128]{1,0:T(8,128)} %all-reduce.10.cloned.1.call-done) | copy-start | bytes 589828
  644.1 226.3 %all-reduce.14.cloned.1.call-start = ((), (), s32[]{:S(2)}) async-start(), calls=%async_computation.3 | async-start | bytes 196608 | tf_op jit(solution)/shard_map/psum | solution.py:190
Sparse Core Ops, SparseCore 0:
  356.5 145.2 all-reduce.7
  504.6 63.8 all-reduce.9
  644.2 154.8 all-reduce.11
  808.3 62.0 all-reduce.13
where the time goes:
time: 879 us; the launch traced here: 878 us
  blocking collectives  457 us (52%)
  waiting for transfers between devices  354 us (40%)
  matrix products  21.3 us (2%)
  other arithmetic  19.7 us (2%)
  between operations  13.5 us (2%)
  local copies, waits for them, and re-layouts  13.4 us (2%)
    psum x1, blocking collectives, body(): full_qkv = lax.psum(partial_qkv, 'seq').astype(jnp.bfloat16)  165 us
    psum x1, waiting for transfers between devices, body(): lax.psum(jnp.dot(second_normed, w_up, preferred_element_type=jnp.float32)...  155 us
    psum x1, blocking collectives, body(): lax.psum((jnp.sum(token_float, 1), jnp.sum(token_float * token_float, 1))...  73.8 us
    pmax x1, blocking collectives, body(): global_top = lax.pmax(local_part[0], 'seq')  73.7 us
    psum x1, blocking collectives, body(): lax.psum((local_part[1] * factor, local_part[2] * factor[..., None]), 'seq')  72.8 us
    psum x1, waiting for transfers between devices, body(): lax.psum((local_part[1] * factor, local_part[2] * factor[..., None]), 'seq')  72.5 us
    psum x1, blocking collectives, body(): lax.psum((jnp.sum(hidden_state, 1), jnp.sum(hidden_state * hidden_state,...  71.2 us
    psum x1, waiting for transfers between devices, body(): lax.psum(jnp.dot(attended, w_out, preferred_element_type=jnp.float32), 'tp')  63.9 us
  transfers between devices with their start and end apart: 4, of which 4 were waited for; matrix products, arithmetic and copies ran while one was open for 0% of the time, Pallas kernels for 0%

commit v1 on v0

--- a/solution.py
+++ b/solution.py
@@ -61,7 +61,7 @@
     normed = finish_norm(token_float, first_sums[0], first_sums[1], ln_first_gain)
     w_flat = w_qkv.reshape(w_qkv.shape[0], 3 * feat_width)
     partial_qkv = jnp.dot(normed, w_flat, preferred_element_type=jnp.float32)
-    full_qkv = lax.psum(partial_qkv, "seq").astype(jnp.bfloat16)
+    full_qkv = jnp.sum(lax.all_gather(partial_qkv, "seq"), axis=0).astype(jnp.bfloat16)
     query = full_qkv[:, :feat_width]
     own_slice = lax.dynamic_slice_in_dim(full_qkv, seq_index * home_rows, home_rows, 0)
     key_new = own_slice[:, feat_width : 2 * feat_width]

time: 879 us -> 1210 us (1.38)
  waiting for transfers between devices: 354 us -> 825 us
  blocking collectives: 457 us -> 290 us
  other arithmetic: 19.7 us -> 43 us
    all_gather x0 -> x1, waiting for transfers between devices: none -> 469 us  [body(): lax.all_gather(partial_qkv, 'seq')]
    psum x1 -> x0, blocking collectives: 165 us -> none  [body(): full_qkv = lax.psum(partial_qkv, 'seq').astype(jnp.bfloat16)]
    reduce_sum x0 -> x1, other arithmetic: none -> 23.7 us  [body(): jnp.sum(lax.all_gather(partial_qkv, 'seq'), axis=0).astype(jnp.bfloat16)]
  transfers between devices with their start and end apart: 4 -> 5, of which waited for: 4 -> 5; matrix products, arithmetic and copies ran while one was open for 0% -> 1% of each run, Pallas kernels for 0% -> 0%
where the time goes in v1:
time: 1210 us
  waiting for transfers between devices  825 us (68%)
  blocking collectives  290 us (24%)
  other arithmetic  43 us (4%)
  matrix products  28.6 us (2%)
  between operations  13.5 us (1%)
    all_gather x1, waiting for transfers between devices, body(): lax.all_gather(partial_qkv, 'seq')  469 us
    psum x1, waiting for transfers between devices, body(): lax.psum(jnp.dot(second_normed, w_up, preferred_element_type=jnp.float32)...  155 us
    psum x1, waiting for transfers between devices, body(): lax.psum((local_part[1] * factor, local_part[2] * factor[..., None]), 'seq')  74.7 us
    psum x1, blocking collectives, body(): lax.psum((jnp.sum(token_float, 1), jnp.sum(token_float * token_float, 1))...  73.8 us
    psum x1, blocking collectives, body(): lax.psum((local_part[1] * factor, local_part[2] * factor[..., None]), 'seq')  72.6 us
    pmax x1, blocking collectives, body(): global_top = lax.pmax(local_part[0], 'seq')  72.3 us
    psum x1, blocking collectives, body(): lax.psum((jnp.sum(hidden_state, 1), jnp.sum(hidden_state * hidden_state,...  71.2 us
    psum x1, waiting for transfers between devices, body(): lax.psum(jnp.dot(attended, w_out, preferred_element_type=jnp.float32), 'tp')  63.9 us
  transfers between devices with their start and end apart: 5, of which 5 were waited for; matrix products, arithmetic and copies ran while one was open for 1% of the time, Pallas kernels for 0%

profile of v1, /device:TPU:8, one launch (start us, length us, event | category | flops | bytes accessed | tf_op | source)
XLA Modules:
  0.0 1209.1 jit_solution(10604268702318646172)
XLA Ops:
  6.6 1.1 convert_reduce_fusion
  7.7 1.2 copy.122
  9.6 73.8 %all-reduce.1 = (f32[384]{0:T(512)S(1)}, f32[384]{0:T(512)S(1)}) all-reduce(f32[384]{0:T(512)S(1)} %get-tuple-element.12, f32[384]{0:T(512)S(1)} %get-tuple-element.11), channel_id=1, replica_groups=mesh['seq'=32,'tp'=8] {'seq'}, use_global_device_ids=true, to_apply=%region_3.0 | all-reduce | flops 768 | bytes 6144 | tf_op jit(solution)/shard_map/psum | solution.py:60
  83.4 2.9 fusion.48
  86.6 2.5 sort.34
  90.1 2.5 sort.35
  96.1 469.0 %all-gather.3.cloned.1.call-done = f32[12288,1536]{1,0:T(8,128)} async-done(((f32[384,1536]{1,0:T(8,128)}), f32[12288,1536]{1,0:T(8,128)}) %all-gather.3.cloned.1.call-update) | async-done | bytes 75497488 | tf_op jit(solution)/shard_map/all_gather | solution.py:64
  565.1 23.7 %reduce_sum.83 = bf16[384,1536]{1,0:T(8,128)(2,1)S(1)} reduce(f32[32,384,1536]{2,1,0:T(8,128)} %bitcast.1, f32[]{:T(128)} %constant.49.clone.1), dimensions={0}, to_apply=%region_4.0 | reduce | flops 18284544 | bytes 76677120 | tf_op jit(solution)/shard_map/reduce_sum | solution.py:64
  592.8 5.4 select_reduce_fusion
  599.7 72.3 %pmax.7 = f32[384,4]{0,1:T(4,128)S(1)} all-reduce(f32[384,4]{0,1:T(4,128)S(1)} %max.18), channel_id=1, replica_groups=mesh['seq'=32,'tp'=8] {'seq'}, use_global_device_ids=true, to_apply=%region_11.12 | all-reduce | flops 1536 | bytes 12288 | tf_op jit(solution)/shard_map/pmax | solution.py:173
  672.4 3.0 fusion.16
  676.9 4.4 fusion.27
  681.4 1.3 gather_fusion.2
  683.5 1.5 add_multiply_fusion
  685.1 72.6 %psum.66 = f32[384,4]{0,1:T(4,128)S(1)} all-reduce(f32[384,4]{0,1:T(4,128)S(1)} %get-tuple-element.17), channel_id=1, replica_groups=mesh['seq'=32,'tp'=8] {'seq'}, use_global_device_ids=true, to_apply=%region_16.17 | all-reduce | flops 1536 | bytes 12288 | tf_op jit(solution)/shard_map/psum | solution.py:175
  757.6 74.7 %all-reduce.7.cloned.1.call-done = f32[384,4,128]{2,0,1:T(8,128)} async-done(((f32[384,4,128]{2,0,1:T(8,128)}), f32[384,4,128]{2,0,1:T(8,128)}) %all-reduce.7.cloned.1.call-update) | async-done | bytes 786448 | tf_op jit(solution)/shard_map/psum | solution.py:175
  832.3 1.4 divide_convert_fusion
  835.1 63.9 %all-reduce.9.cloned.1.call-done = f32[384,128]{1,0:T(8,128)} async-done(((f32[384,128]{1,0:T(8,128)}), f32[384,128]{1,0:T(8,128)}) %all-reduce.9.cloned.1.call-update) | async-done | bytes 196624 | tf_op jit(solution)/shard_map/psum | solution.py:181
  900.1 71.2 %all-reduce = (f32[384]{0:T(512)S(1)}, f32[384]{0:T(512)S(1)}) all-reduce(f32[384]{0:T(512)S(1)} %get-tuple-element.10, f32[384]{0:T(512)S(1)} %get-tuple-element.9), channel_id=1, replica_groups=mesh['seq'=32,'tp'=8] {'seq'}, use_global_device_ids=true, to_apply=%region_21.22 | all-reduce | flops 768 | bytes 6144 | tf_op jit(solution)/shard_map/psum | solution.py:183
  971.2 3.3 fusion.47
  974.8 154.9 %all-reduce.11.cloned.1.call-done = f32[384,2048]{1,0:T(8,128)} async-done(((f32[384,2048]{1,0:T(8,128)}), f32[384,2048]{1,0:T(8,128)}) %all-reduce.11.cloned.1.call-update) | async-done | bytes 3145744 | tf_op jit(solution)/shard_map/psum | solution.py:187
  1129.7 9.0 fusion.32
  1138.7 62.2 %all-reduce.13.cloned.1.call-done = bf16[384,128]{1,0:T(8,128)(2,1)} async-done(((bf16[384,128]{1,0:T(8,128)(2,1)}), bf16[384,128]{1,0:T(8,128)(2,1)}) %all-reduce.13.cloned.1.call-update) | async-done | bytes 98320 | tf_op jit(solution)/shard_map/psum | solution.py:190
  1201.0 1.6 add_convert_fusion
  (110 shorter events, 16.1 us)
Async XLA Ops:
  6.5 584.1 %copy-start = (bf16[3,256,512]{2,1,0:T(8,128)(2,1)S(1)}, bf16[3,256,512]{2,1,0:T(8,128)(2,1)}, u32[]{:S(2)}) copy-start(bf16[3,256,512]{2,1,0:T(8,128)(2,1)} %param.23) | copy-start | bytes 2359300
  6.5 79.8 %copy-start.13 = (s32[96]{0:T(128)S(1)}, s32[96]{0:T(128)}, u32[]{:S(2)}) copy-start(s32[96]{0:T(128)} %param.25) | copy-start | bytes 1156
  6.5 79.8 %copy-start.9 = (s32[8]{0:T(128)S(1)}, s32[8]{0:T(128)}, u32[]{:S(2)}) copy-start(s32[8]{0:T(128)} %param.26) | copy-start | bytes 100
  6.5 79.9 %copy-start.12 = (s32[96]{0:T(128)S(1)}, s32[96]{0:T(128)}, u32[]{:S(2)}) copy-start(s32[96]{0:T(128)} %param.27) | copy-start | bytes 1156
  6.5 558.6 %all-gather.3.cloned.1.call-start = ((), (), s32[]{:S(2)}) async-start(), calls=%async_computation.4 | async-start | bytes 77856768 | tf_op jit(solution)/shard_map/all_gather | solution.py:64
  86.2 746.1 %all-reduce.7.cloned.1.call-start = ((), (), s32[]{:S(2)}) async-start(), calls=%async_computation | async-start | bytes 1572864 | tf_op jit(solution)/shard_map/psum | solution.py:175
  93.2 2.1 copy-start.5
  592.7 79.3 %copy-start.8 = (pred[4,4]{0,1:T(4,128)(4,1)S(1)}, pred[4,4]{0,1:T(4,128)(4,1)}, u32[]{:S(2)}) copy-start(pred[4,4]{0,1:T(4,128)(4,1)} %iota_compare_fusion.2) | copy-start | bytes 52
  592.7 79.3 %copy-start.7 = (pred[3,256]{1,0:T(4,128)(4,1)S(1)}, pred[3,256]{1,0:T(4,128)(4,1)}, u32[]{:S(2)}) copy-start(pred[3,256]{1,0:T(4,128)(4,1)} %iota_compare_fusion) | copy-start | bytes 2308
  592.7 79.6 %copy-start.6 = (f32[4]{0:T(128)S(1)}, f32[4]{0:T(128)}, u32[]{:S(2)}) copy-start(f32[4]{0:T(128)} %copy-done.5) | copy-start | bytes 52
  598.2 78.2 %copy-start.10 = (bf16[3,256,512]{2,1,0:T(8,128)(2,1)S(1)}, bf16[3,256,512]{2,1,0:T(8,128)(2,1)}, u32[]{:S(2)}) copy-start(bf16[3,256,512]{2,1,0:T(8,128)(2,1)} %param.24) | copy-start | bytes 2359300
  682.9 151.1 %copy-start.4 = (bf16[512,128]{1,0:T(8,128)(2,1)S(1)}, bf16[512,128]{1,0:T(8,128)(2,1)}, u32[]{:S(2)}) copy-start(bf16[512,128]{1,0:T(8,128)(2,1)} %param.17) | copy-start | bytes 393220
  683.2 151.8 %copy-start.14 = (bf16[128]{0:T(256)(128)(2,1)S(1)}, bf16[128]{0:T(256)(128)(2,1)}, u32[]{:S(2)}) copy-start(bf16[128]{0:T(256)(128)(2,1)} %param.18) | copy-start | bytes 772
  683.2 215.7 %copy-start.1 = (bf16[384,128]{1,0:T(8,128)(2,1)S(1)}, bf16[384,128]{1,0:T(8,128)(2,1)}, u32[]{:S(2)}) copy-start(bf16[384,128]{1,0:T(8,128)(2,1)} %param.14) | copy-start | bytes 294916
  683.5 287.8 %copy-start.3 = (bf16[128,2048]{1,0:T(8,128)(2,1)S(1)}, bf16[128,2048]{1,0:T(8,128)(2,1)}, u32[]{:S(2)}) copy-start(bf16[128,2048]{1,0:T(8,128)(2,1)} %param.19) | copy-start | bytes 1572868
  685.0 213.9 %all-reduce.9.cloned.1.call-start = ((), (), s32[]{:S(2)}) async-start(), calls=%async_computation.1 | async-start | bytes 393216 | tf_op jit(solution)/shard_map/psum | solution.py:181
  835.0 294.7 %all-reduce.11.cloned.1.call-start = ((), (), s32[]{:S(2)}) async-start(), calls=%async_computation.2 | async-start | bytes 6291456 | tf_op jit(solution)/shard_map/psum | solution.py:187
  971.2 158.4 %copy-start.11 = (bf16[2048,128]{1,0:T(8,128)(2,1)S(1)}, bf16[2048,128]{1,0:T(8,128)(2,1)}, u32[]{:S(2)}) copy-start(bf16[2048,128]{1,0:T(8,128)(2,1)} %param.20) | copy-start | bytes 1572868
  974.6 226.4 %copy-start.2 = (f32[384,128]{1,0:T(8,128)S(1)}, f32[384,128]{1,0:T(8,128)}, u32[]{:S(2)}) copy-start(f32[384,128]{1,0:T(8,128)} %all-reduce.9.cloned.1.call-done) | copy-start | bytes 589828
  974.6 226.4 %all-reduce.13.cloned.1.call-start = ((), (), s32[]{:S(2)}) async-start(), calls=%async_computation.3 | async-start | bytes 196608 | tf_op jit(solution)/shard_map/psum | solution.py:190
Sparse Core Ops, SparseCore 0:
  86.4 478.6 all-gather.2
  685.1 147.1 all-reduce.6
  835.1 63.8 all-reduce.8
  974.7 154.9 all-reduce.10
  1138.9 62.0 all-reduce.12
